TPU v7x, 256 devices: a whole 4x4x8 slice. The times are simulated.
256 devices in a mesh: req: 64 (over y, z_lo, x, core), tp: 4 (over z_hi).
Axes of the slice: x: 4, y: 4, z: 8 (z_hi: 4, z_lo: 2; z = z_hi * 2 + z_lo), core: 2. Of those that a mesh axis runs over, the one named last changes fastest.
Arguments:
- tokens: bfloat16 [16384, 2048], P('req'), may hold values from -6 to 6
- norm_gain: float32 [2048], replicated, may hold values from 0.25 to 1.75
- w_query: bfloat16 [2048, 2048], P(None, 'tp'), may hold values from -1 to 1
- w_key: bfloat16 [2048, 2048], P(None, 'tp'), may hold values from -1 to 1
- w_value: bfloat16 [2048, 2048], P(None, 'tp'), may hold values from -0.125 to 0.125
- w_out: bfloat16 [2048, 2048], P('tp'), may hold values from -0.125 to 0.125
- lambdas: float32 [4, 8, 128], P(None, 'tp'), may hold values from -1 to 1
- sub_gain: float32 [8, 256], P('tp'), may hold values from 0.5 to 2
- lengths: int32 [4], replicated, may hold values from 1 to 8192, 16384 in all
Outputs:
- hidden: bfloat16 [16384, 2048], P('req')
- key_cache: bfloat16 [16384, 2048], P('req', 'tp')
- value_cache: bfloat16 [16384, 2048], P('req', 'tp')
Inputs may be any that keep to these rules, and one draw needn't show every extreme that they name: The lengths sum to 16384; the longest is exactly 8192.
All inputs are finite; a program needn't handle non-finite values.
Results may differ from a plain program's by a relative error of at most 0.007.
Values may be sent and summed in bfloat16 or wider, within the bound.
No kernel may reach another device: no remote copies, remote signals or barrier semaphores. Data moves between devices by JAX's collectives and lax.ppermute only.
A program may use at most 128 MiB of HBM per device.

v0:
```python
import math
import jax
import jax.numpy as jnp
from jax import lax
from jax.sharding import Mesh
from jax.sharding import PartitionSpec as P

QK = 128
VD = 256
MAXLEN = 8192
lambda_start = 0.8 - 0.6 * math.exp(-3.3)
masked_score = -1e30


def locate(index, lengths):
    ends = jnp.cumsum(lengths)
    starts = ends - lengths
    segment = jnp.sum((ends[None, :] <= index[:, None]).astype(jnp.int32), axis=1)
    hit = jnp.arange(lengths.shape[0], dtype=jnp.int32)[None, :] == segment[:, None]
    begin = jnp.sum(jnp.where(hit, starts[None, :], 0), axis=1)
    return (segment, index - begin)


def rotate(proj, position):
    half = proj.shape[-1] // 2
    freq = 10000.0 ** (-jnp.arange(half, dtype=jnp.float32) / half)
    angle = position.astype(jnp.float32)[:, None] * freq[None, :]
    cosine = jnp.cos(angle)[:, None, None, :]
    sine = jnp.sin(angle)[:, None, None, :]
    front = proj[..., :half]
    back = proj[..., half:]
    return jnp.concatenate([front * cosine - back * sine, back * cosine + front * sine], axis=-1)


def swap_cores(value):
    return lax.ppermute(value, "core", [(0, 1), (1, 0)])


def on_device(tokens, norm_gain, w_query, w_key, w_value, w_out, lambdas, sub_gain, lengths):
    rows = tokens.shape[0]
    heads = w_query.shape[1] // (2 * QK)
    key_cols = heads * 2 * QK
    ys, zs, xs = (lax.axis_size("y"), lax.axis_size("z"), lax.axis_size("x"))
    chips = ys * zs * xs
    total = rows * 2 * chips
    core = lax.axis_index("core")
    chip = (lax.axis_index("y") * zs + lax.axis_index("z")) * xs + lax.axis_index("x")
    first = (chip * 2 + core) * rows
    local_index = first + jnp.arange(rows, dtype=jnp.int32)
    unused, pos_own = locate(local_index, lengths)
    xf = tokens.astype(jnp.float32)
    normed = (xf * lax.rsqrt(jnp.mean(xf * xf, axis=-1, keepdims=True) + 1e-06) * norm_gain).astype(
        jnp.bfloat16
    )
    keys = rotate(
        jnp.dot(normed, w_key, preferred_element_type=jnp.float32).reshape(rows, heads, 2, QK),
        pos_own,
    ).astype(jnp.bfloat16)
    values = jnp.dot(normed, w_value, preferred_element_type=jnp.float32).astype(jnp.bfloat16)
    key_flat = keys.reshape(rows, key_cols)
    lam = (
        jnp.exp(jnp.sum(lambdas[0] * lambdas[1], axis=-1))
        - jnp.exp(jnp.sum(lambdas[2] * lambdas[3], axis=-1))
        + lambda_start
    )
    scale = QK ** (-0.5)

    def head_kv(h):
        k_h = lax.dynamic_index_in_dim(keys, h, axis=1, keepdims=False).reshape(rows, 2 * QK)
        v_h = lax.dynamic_index_in_dim(values.reshape(rows, heads, VD), h, axis=1, keepdims=False)
        return jnp.concatenate([k_h, v_h], axis=1)

    def in_order(mine, theirs, first_is_mine):
        rows_each = mine.shape[0]
        both = jnp.zeros((2 * rows_each,) + mine.shape[1:], mine.dtype)
        both = lax.dynamic_update_slice_in_dim(
            both, mine, jnp.where(first_is_mine, 0, rows_each), axis=0
        )
        return lax.dynamic_update_slice_in_dim(
            both, theirs, jnp.where(first_is_mine, rows_each, 0), axis=0
        )

    span = 2 * rows
    z = lax.axis_index("z")
    kv_both = jnp.stack([head_kv(0), head_kv(1)], axis=1)
    halves = [
        lax.ppermute(kv_both[..., i * 2 * QK : (i + 1) * 2 * QK], "z", [(0, 1), (1, 0)])
        for i in range(2)
    ]
    kv_chips = in_order(kv_both, jnp.concatenate(halves, axis=-1), z == 0)
    mine = lax.dynamic_index_in_dim(kv_chips, core, axis=1, keepdims=False).reshape(2, rows, -1)
    theirs = swap_cores(
        lax.dynamic_index_in_dim(kv_chips, 1 - core, axis=1, keepdims=False)
    ).reshape(2, rows, -1)
    quad = jnp.zeros((2, span, mine.shape[-1]), mine.dtype)
    quad = lax.dynamic_update_slice_in_dim(quad, mine, core * rows, axis=1)
    quad = lax.dynamic_update_slice_in_dim(quad, theirs, (1 - core) * rows, axis=1)
    kv_quad = quad.reshape(2 * span, -1)
    kv_pair = lax.dynamic_index_in_dim(quad, z, axis=0, keepdims=False)
    gathered = lax.all_gather(kv_quad, ("y", "x"), axis=0, tiled=True)
    query = rotate(
        jnp.dot(normed, w_query, preferred_element_type=jnp.float32).reshape(rows, heads, 2, QK),
        pos_own,
    ).astype(jnp.bfloat16)
    q_pair = in_order(
        lax.dynamic_index_in_dim(query, core, axis=1, keepdims=False),
        swap_cores(lax.dynamic_index_in_dim(query, 1 - core, axis=1, keepdims=False)),
        core == 0,
    )
    reach = min(MAXLEN // span, chips - 1)
    window = reach * span
    base = chip * span
    first_chip = jnp.clip(chip - reach, 0, chips - reach)
    start = first_chip * span
    q_index = base + jnp.arange(span, dtype=jnp.int32)
    q_seg, unused = locate(q_index, lengths)

    def stats_of(kv_win, key_index, allowed):
        v_win = kv_win[:, 2 * QK :]
        stats = []
        for m in range(2):
            k_m = kv_win[:, m * QK : (m + 1) * QK]
            scores = (
                jnp.einsum("qd,kd->qk", q_pair[:, m, :], k_m, preferred_element_type=jnp.float32)
                * scale
            )
            scores = jnp.where(allowed, scores, masked_score)
            top = jnp.max(scores, axis=-1, keepdims=True)
            weights = jnp.where(allowed, jnp.exp(scores - top), 0.0)
            mass = jnp.sum(weights, axis=-1, keepdims=True)
            acc = jnp.dot(weights.astype(jnp.bfloat16), v_win, preferred_element_type=jnp.float32)
            stats.append((top, mass, acc))
        return stats

    local_allowed = (q_index[None, :] <= q_index[:, None]) & (q_seg[None, :] == q_seg[:, None])
    local_stats = stats_of(kv_pair, q_index, local_allowed)
    local_stats, gathered = lax.optimization_barrier((local_stats, gathered))
    c = first_chip + jnp.arange(reach, dtype=jnp.int32)
    slot = (c // (zs * xs) * xs + c % xs) * zs + c // xs % zs
    kv_window = jnp.take(gathered.reshape(chips, span, -1), slot, axis=0, mode="clip").reshape(
        window, -1
    )
    pieces = 2
    piece = window // pieces

    def part(p):
        key_index = start + p * piece + jnp.arange(piece, dtype=jnp.int32)
        k_seg, unused = locate(key_index, lengths)
        allowed = (key_index[None, :] < base) & (k_seg[None, :] == q_seg[:, None])
        return stats_of(kv_window[p * piece : (p + 1) * piece], key_index, allowed)

    all_stats = [local_stats] + [part(p) for p in range(pieces)]

    def attend(m):
        tops = [stats[m][0] for stats in all_stats]
        top = tops[0]
        for other in tops[1:]:
            top = jnp.maximum(top, other)
        acc = 0.0
        mass = 0.0
        for stats in all_stats:
            fade = jnp.exp(stats[m][0] - top)
            mass = mass + stats[m][1] * fade
            acc = acc + stats[m][2] * fade
        return acc / mass

    lam_h = lax.dynamic_index_in_dim(lam, core, keepdims=False)
    gain_h = lax.dynamic_index_in_dim(sub_gain, core, axis=0, keepdims=False)
    diff = attend(0) - lam_h * attend(1)
    head_out = (
        diff
        * lax.rsqrt(jnp.mean(diff * diff, axis=-1, keepdims=True) + 1e-05)
        * gain_h
        * (1.0 - lambda_start)
    ).astype(jnp.bfloat16)
    own_rows = lax.dynamic_slice_in_dim(head_out, core * rows, rows, axis=0)
    other_rows = swap_cores(lax.dynamic_slice_in_dim(head_out, (1 - core) * rows, rows, axis=0))
    merged = jnp.where(
        core == 0,
        jnp.concatenate([own_rows, other_rows], axis=1),
        jnp.concatenate([other_rows, own_rows], axis=1),
    )
    summed = lax.psum(
        jnp.dot(merged, w_out, preferred_element_type=jnp.float32).astype(jnp.bfloat16), "tp"
    ).astype(jnp.float32)
    hidden = (xf + summed).astype(jnp.bfloat16)
    return (hidden, key_flat, values)


def solution(mesh):
    req, tp = (mesh.shape["req"], mesh.shape["tp"])
    paired = Mesh(mesh.devices.reshape(req // 16, 2, 4, 2, tp), ("y", "z", "x", "core", "tp"))
    rows = ("y", "z", "x", "core")
    in_specs = (
        P(rows, None),
        P(),
        P(None, "tp"),
        P(None, "tp"),
        P(None, "tp"),
        P("tp", None),
        P(None, "tp", None),
        P("tp", None),
        P(),
    )
    out_specs = (P(rows, None), P(rows, "tp"), P(rows, "tp"))
    return jax.shard_map(
        on_device, mesh=paired, in_specs=in_specs, out_specs=out_specs, check_vma=False
    )
```

profile of v0, /device:TPU:1, one launch (start us, length us, event | category | flops | bytes accessed | tf_op | source)
XLA Modules:
  0.0 296.7 jit_solution(17206890886922927815)
XLA Ops:
  7.3 1.0 reduce-window.8
  8.2 0.7 bitcast_subtract_fusion
  9.1 1.5 fusion.16
  10.6 2.7 fusion.131
  13.3 0.3 reshape.337
  13.7 0.5 multiply_cosine_fusion
  14.2 0.8 multiply_subtract_fusion
  15.0 0.7 maximum_convert_fusion
  15.7 0.8 fusion.136
  16.6 2.7 convolution_convert_fusion.1
  19.3 0.7 copy-done.6
  20.1 0.4 fusion.137
  20.4 0.9 copy.47
  21.5 0.8 fusion.103
  22.2 2.5 collective-permute-start.1
  24.8 5.1 %collective-permute-done.1 = bf16[256,2,256]{2,0,1:T(8,128)(2,1)S(1)} collective-permute-done((bf16[256,2,256]{2,0,1:T(8,128)(2,1)}, bf16[256,2,256]{2,0,1:T(8,128)(2,1)S(1)}, u32[]{:S(2)}, u32[]{:S(2)}) %collective-permute-start.1) | collective-permute-done | bytes 262176 | tf_op jit(solution)/shard_map/ppermute | solution.py:87
  30.0 5.5 %collective-permute-done.2 = bf16[256,2,256]{2,0,1:T(8,128)(2,1)} collective-permute-done((bf16[256,2,256]{2,0,1:T(8,128)(2,1)S(1)}, bf16[256,2,256]{2,0,1:T(8,128)(2,1)}, u32[]{:S(2)}, u32[]{:S(2)}) %collective-permute-start.2) | collective-permute-done | bytes 262176 | tf_op jit(solution)/shard_map/ppermute | solution.py:87
  35.5 1.0 maximum_dynamic-update-slice_fusion
  36.5 1.0 dynamic-slice_bitcast_fusion.1
  37.5 2.4 collective-permute-start.3
  40.0 1.1 constant_dynamic-update-slice_fusion.1
  41.1 0.7 collective-permute-done.3
  41.8 1.1 constant_dynamic-update-slice_fusion
  42.9 1.0 copy-done.1
  43.9 3.6 %fusion.133 = f32[256,512]{1,0:T(8,128)} fusion(bf16[2048,512]{1,0:T(8,128)(2,1)} %param.11, bf16[256,2048]{1,0:T(8,128)(2,1)} %param.9, f32[2048]{0:T(1024)S(1)} %copy-done.16, f32[256]{0:T(256)S(1)} %add_rsqrt_fusion.1), kind=kOutput, calls=%fused_computation.180 | convolution fusion | flops 538968064 | bytes 3679232 | tf_op jit(solution)/shard_map/dot_general | solution.py:102
  47.5 2.2 reshape.336
  49.7 2.0 add_convert_fusion
  51.7 0.7 fusion.113
  52.4 0.7 copy.49
  53.1 0.4 collective-permute-start
  53.5 0.6 broadcast_compare_fusion.1
  54.1 0.6 pad_clamp_fusion
  54.7 0.6 broadcast_compare_fusion
  55.4 0.6 iota_add_fusion
  56.0 1.3 convert_reduce_fusion.2
  57.3 0.5 subtract_add_fusion
  57.9 0.7 copy-done.7
  58.6 0.7 constant_dynamic-slice_fusion.2
  59.3 1.2 dynamic_slice.55
  60.4 0.9 convert_reduce_fusion.1
  61.3 1.6 constant_dynamic-update-slice_fusion.2
  63.0 1.3 fusion.139
  64.3 1.3 fusion.138
  65.6 0.4 fusion.93
  66.1 0.5 fusion.95
  66.6 1.4 fusion.97
  68.0 94.9 %all-gather.2.cloned.1.call-done = bf16[16384,512]{1,0:T(8,128)(2,1)} async-done(((bf16[1024,512]{1,0:T(8,128)(2,1)}), bf16[16384,512]{1,0:T(8,128)(2,1)}) %all-gather.2.cloned.1.call-update) | async-done | bytes 16777232 | tf_op jit(solution)/shard_map/all_gather | solution.py:100
  162.8 10.7 %gather_fusion = bf16[16,512,512]{2,1,0:T(8,128)(2,1)} fusion(bf16[32,512,512]{2,1,0:T(8,128)(2,1)} %bitcast.87, s32[1024]{0:T(1024)} %pad_clamp_fusion), kind=kCustom, calls=%fused_computation | custom fusion | bytes 16777280 | tf_op jit(solution)/shard_map/jit(_take)/gather | solution.py:140
  173.5 3.9 %fusion.135 = (bf16[8,512,512]{2,1,0:T(8,128)(2,1)S(1)}, bf16[8,512,512]{2,1,0:T(8,128)(2,1)S(1)}) fusion(bf16[16,512,512]{2,1,0:T(8,128)(2,1)} %gather_fusion), kind=kLoop, calls=%fused_computation.181 | loop fusion | bytes 16777216 | tf_op jit(solution)/shard_map/slice | solution.py:150
  177.4 2.4 fusion.142
  179.8 2.4 fusion.141
  182.2 4.6 %fusion.143 = (f32[512]{0:T(512)S(1)}, f32[512,4096]{1,0:T(8,128)}) fusion(bf16[4096,512]{1,0:T(8,128)(2,1)S(1)} %bitcast.92, bf16[512,2,128]{2,0,1:T(8,128)(2,1)S(1)} %copy-done.8, s32[512]{0:T(512)S(1)} %copy-done.9, s32[4096]{0:T(1024)S(1)} %get-tuple-element.28, pred[4096]{0:T(1024)(128)(4,1)S(1)} %copy-done.13), kind=kOutput, calls=%fused_computation.189 | convolution fusion | flops 547356160 | bytes 9592832 | tf_op jit(solution)/shard_map/qd,kd->qk/dot_general | solution.py:124
  186.8 3.6 %fusion.140 = (f32[512]{0:T(512)S(1)}, f32[512,4096]{1,0:T(8,128)S(1)}) fusion(bf16[4096,512]{1,0:T(8,128)(2,1)} %bitcast.93, bf16[512,2,128]{2,0,1:T(8,128)(2,1)S(1)} %copy-done.8, s32[512]{0:T(512)S(1)} %copy-done.9, s32[4096]{0:T(1024)S(1)} %get-tuple-element.28, pred[4096]{0:T(1024)(128)(4,1)S(1)} %copy-done.13), kind=kOutput, calls=%fused_computation.186 | convolution fusion | flops 547356160 | bytes 9592832 | tf_op jit(solution)/shard_map/qd,kd->qk/dot_general | solution.py:124
  190.4 11.0 %fusion.4 = (f32[512]{0:T(512)S(1)}, f32[512]{0:T(512)S(1)}, f32[512]{0:T(512)S(1)}, f32[512]{0:T(512)S(1)}) fusion(f32[512,4096]{1,0:T(8,128)S(1)} %get-tuple-element.64, f32[512]{0:T(512)S(1)} %get-tuple-element.63, s32[4096]{0:T(1024)S(1)} %get-tuple-element.27, s32[512]{0:T(512)S(1)} %copy-done.9, pred[4096]{0:T(1024)(128)(4,1)S(1)} %copy-done.12, ...), kind=kLoop, calls=%fused_computation.15 | loop fusion | flops 33552384 | bytes 33613824 | tf_op jit(solution)/shard_map/reduce_sum | solution.py:130
  201.4 5.6 %fusion.61 = f32[512,256]{1,0:T(8,128)S(1)} fusion(bf16[4096,512]{1,0:T(8,128)(2,1)} %bitcast.94, f32[512,4096]{1,0:T(8,128)} %get-tuple-element.68, f32[512]{0:T(512)S(1)} %get-tuple-element.67, s32[4096]{0:T(1024)S(1)} %get-tuple-element.28, s32[512]{0:T(512)S(1)} %copy-done.9, pred[4096]{0:T(1024)(128)(4,1)S(1)} %copy-done.13, f32[512]{0:T(512)S(1)} %bitcast.124), kind=kOutput, calls=%fused_computation.46 | convolution fusion | flops 1084358656 | bytes 11036672 | tf_op jit(solution)/shard_map/dot_general | solution.py:131
  207.1 3.9 %fusion.41 = f32[512,256]{1,0:T(8,128)S(1)} fusion(bf16[4096,512]{1,0:T(8,128)(2,1)} %bitcast.95, f32[512,4096]{1,0:T(8,128)S(1)} %get-tuple-element.62, f32[512]{0:T(512)S(1)} %get-tuple-element.61, s32[4096]{0:T(1024)S(1)} %get-tuple-element.28, s32[512]{0:T(512)S(1)} %copy-done.9, pred[4096]{0:T(1024)(128)(4,1)S(1)} %copy-done.13, f32[512]{0:T(512)S(1)} %bitcast.123), kind=kOutput, calls=%fused_computation.42 | convolution fusion | flops 1084358656 | bytes 11036672 | tf_op jit(solution)/shard_map/dot_general | solution.py:131
  211.1 2.4 fusion.85
  213.4 3.1 %multiply_reduce_fusion = (f32[512]{0:T(512)S(1)}, f32[512,256]{1,0:T(8,128)S(1)}) fusion(f32[512,256]{1,0:T(8,128)S(1)} %fusion.85, f32[512]{0:T(512)S(1)} %bitcast.117, f32[512,256]{1,0:T(8,128)S(1)} %fusion.61, f32[512]{0:T(512)S(1)} %bitcast.119, bf16[4096,512]{1,0:T(8,128)(2,1)S(1)} %bitcast.91, f32[512,4096]{1,0:T(8,128)S(1)} %get-tuple-element.64, ...), kind=kOutput, calls=%fused_computation.74 | convolution fusion | flops 1085406720 | bytes 12615684 | tf_op jit(solution)/shard_map/dot_general | solution.py:131
  216.7 0.8 collective-permute-start.4
  217.5 1.0 collective-permute-done.4
  218.5 1.7 convolution_convert_fusion
  220.2 0.8 convert_element_type.86
  221.0 66.2 %all-reduce.2.cloned.1.call-done = bf16[256,2048]{1,0:T(8,128)(2,1)} async-done(((bf16[256,2048]{1,0:T(8,128)(2,1)}), bf16[256,2048]{1,0:T(8,128)(2,1)}) %all-reduce.2.cloned.1.call-update) | async-done | bytes 1048592 | tf_op jit(solution)/shard_map/psum | solution.py:183
  287.2 2.6 fusion.19
  (64 shorter events, 1.3 us)
Async XLA Ops:
  7.2 211.3 %copy-start = (bf16[512,2048]{1,0:T(8,128)(2,1)S(1)}, bf16[512,2048]{1,0:T(8,128)(2,1)}, u32[]{:S(2)}) copy-start(bf16[512,2048]{1,0:T(8,128)(2,1)} %param.14) | copy-start | bytes 6291460
  7.2 155.7 %all-gather.2.cloned.1.call-start = ((), (), s32[]{:S(2)}) async-start(), calls=%async_computation | async-start | bytes 17825792 | tf_op jit(solution)/shard_map/all_gather | solution.py:100
  8.2 2.4 copy-start.14
  10.6 6.0 %copy-start.16 = (f32[2048]{0:T(1024)S(1)}, f32[2048]{0:T(1024)}, u32[]{:S(2)}) copy-start(f32[2048]{0:T(1024)} %param.10) | copy-start | bytes 24580
  14.2 5.9 %copy-start.5 = (f32[256,64]{1,0:T(8,128)}, f32[256,64]{1,0:T(8,128)S(1)}, u32[]{:S(2)}) copy-start(f32[256,64]{1,0:T(8,128)S(1)} %get-tuple-element.56) | copy-start | bytes 196612
  19.3 0.7 copy-start.6
  22.2 7.8 %collective-permute-start.1 = (bf16[256,2,256]{2,0,1:T(8,128)(2,1)}, bf16[256,2,256]{2,0,1:T(8,128)(2,1)S(1)}, u32[]{:S(2)}, u32[]{:S(2)}) collective-permute-start(bf16[256,2,256]{2,0,1:T(8,128)(2,1)} %get-tuple-element.47), channel_id=1, source_target_pairs={{0,32},{32,0},{1,33},{33,1},{2,34},{34,2},{3,35},{35,3},{4,36},{36... | collective-permute-start | bytes 786440 | tf_op jit(solution)/shard_map/ppermute | solution.py:87
  24.7 10.8 %collective-permute-start.2 = (bf16[256,2,256]{2,0,1:T(8,128)(2,1)S(1)}, bf16[256,2,256]{2,0,1:T(8,128)(2,1)}, u32[]{:S(2)}, u32[]{:S(2)}) collective-permute-start(bf16[256,2,256]{2,0,1:T(8,128)(2,1)S(1)} %get-tuple-element.48), channel_id=1, source_target_pairs={{0,32},{32,0},{1,33},{33,1},{2,34},{34,2},{3,35},{35,3},{4,36},{36... | collective-permute-start | bytes 786440 | tf_op jit(solution)/shard_map/ppermute | solution.py:87
  37.5 4.3 %collective-permute-start.3 = (bf16[512,512]{1,0:T(8,128)(2,1)}, bf16[512,512]{1,0:T(8,128)(2,1)}, u32[]{:S(2)}, u32[]{:S(2)}) collective-permute-start(bf16[512,512]{1,0:T(8,128)(2,1)} %get-tuple-element.39), channel_id=1, source_target_pairs={{0,4},{4,0},{1,5},{5,1},{2,6},{6,2},{3,7},{7,3},{8,12},{12,8},{9,1... | collective-permute-start | bytes 1572872 | tf_op jit(solution)/shard_map/ppermute | solution.py:36
  42.9 1.0 copy-start.1
  43.9 11.4 %copy-start.15 = (f32[4,2,128]{2,1,0:T(2,128)S(1)}, f32[4,2,128]{2,1,0:T(2,128)}, u32[]{:S(2)}) copy-start(f32[4,2,128]{2,1,0:T(2,128)} %param.15) | copy-start | bytes 12292
  43.9 19.1 %copy-start.2 = (bf16[2,512,512]{2,1,0:T(8,128)(2,1)S(1)}, bf16[2,512,512]{2,1,0:T(8,128)(2,1)}, u32[]{:S(2)}) copy-start(bf16[2,512,512]{2,1,0:T(8,128)(2,1)} %copy-done.1) | copy-start | bytes 3145732
  43.9 243.3 %all-reduce.2.cloned.1.call-start = ((), (), s32[]{:S(2)}) async-start(), calls=%async_computation.1 | async-start | bytes 2097152 | tf_op jit(solution)/shard_map/psum | solution.py:183
  53.1 8.3 %collective-permute-start = (bf16[256,2,128]{2,0,1:T(8,128)(2,1)}, bf16[256,2,128]{2,0,1:T(8,128)(2,1)}, u32[]{:S(2)}, u32[]{:S(2)}) collective-permute-start(bf16[256,2,128]{2,0,1:T(8,128)(2,1)} %bitcast.85), channel_id=1, source_target_pairs={{0,4},{4,0},{1,5},{5,1},{2,6},{6,2},{3,7},{7,3},{8,12},{12,8},{9,1... | collective-permute-start | bytes 393224 | tf_op jit(solution)/shard_map/ppermute | solution.py:36
  53.5 4.3 %copy-start.10 = (s32[512]{0:T(512)}, s32[512]{0:T(512)S(1)}, u32[]{:S(2)}) copy-start(s32[512]{0:T(512)S(1)} %iota_add_fusion.2) | copy-start | bytes 6148
  57.9 0.7 copy-start.7
  58.6 7.0 %copy-start.9 = (s32[512]{0:T(512)S(1)}, s32[512]{0:T(512)}, u32[]{:S(2)}) copy-start(s32[512]{0:T(512)} %convert_reduce_fusion.2) | copy-start | bytes 6148
  58.6 7.0 %copy-start.11 = (s32[512]{0:T(512)S(1)}, s32[512]{0:T(512)}, u32[]{:S(2)}) copy-start(s32[512]{0:T(512)} %copy-done.10) | copy-start | bytes 6148
  173.5 3.9 %copy-start.8 = (bf16[512,2,128]{2,0,1:T(8,128)(2,1)S(1)}, bf16[512,2,128]{2,0,1:T(8,128)(2,1)}, u32[]{:S(2)}) copy-start(bf16[512,2,128]{2,0,1:T(8,128)(2,1)} %constant_dynamic-update-slice_fusion.2) | copy-start | bytes 786436
  173.5 3.9 %copy-start.12 = (pred[4096]{0:T(1024)(128)(4,1)S(1)}, pred[4096]{0:T(1024)(128)(4,1)}, u32[]{:S(2)}) copy-start(pred[4096]{0:T(1024)(128)(4,1)} %broadcast_compare_fusion.1) | copy-start | bytes 12292
  177.4 4.8 %copy-start.4 = (bf16[8,512,512]{2,1,0:T(8,128)(2,1)}, bf16[8,512,512]{2,1,0:T(8,128)(2,1)S(1)}, u32[]{:S(2)}) copy-start(bf16[8,512,512]{2,1,0:T(8,128)(2,1)S(1)} %get-tuple-element.38) | copy-start | bytes 12582916
  179.8 2.4 copy-start.13
  207.1 4.0 %copy-start.17 = (f32[512,256]{1,0:T(8,128)S(1)}, f32[512,256]{1,0:T(8,128)}, u32[]{:S(2)}) copy-start(f32[512,256]{1,0:T(8,128)} %fusion.97) | copy-start | bytes 1572868
  216.5 70.7 %copy-start.3 = (bf16[256,2048]{1,0:T(8,128)(2,1)S(1)}, bf16[256,2048]{1,0:T(8,128)(2,1)}, u32[]{:S(2)}) copy-start(bf16[256,2048]{1,0:T(8,128)(2,1)} %param.9) | copy-start | bytes 3145732
  216.7 1.8 collective-permute-start.4
Sparse Core Ops, SparseCore 0:
  44.0 118.7 all-gather.1
  220.3 66.8 all-reduce.1
where the time goes:
time: 297 us
  waiting for transfers between devices  173 us (58%)
  matrix products  43.2 us (15%)
  local copies, waits for them, and re-layouts  30.1 us (10%)
  other arithmetic  29.3 us (10%)
  between operations  14.5 us (5%)
  starting transfers between devices  6.13 us (2%)
    all_gather x1, waiting for transfers between devices, on_device(): gathered = lax.all_gather(kv_quad, ('y', 'x'), axis=0, tiled=True)  94.9 us
    psum x1, waiting for transfers between devices, on_device(): lax.psum(jnp.dot(merged, w_out, preferred_element_type=jnp.float32).astyp...  66.2 us
    dot_general x6, matrix products, stats_of(): jnp.dot(weights.astype(jnp.bfloat16), v_win, preferred_element_type=jnp.f...  17 us
    dot_general x6, matrix products, stats_of(): jnp.einsum('qd,kd->qk', q_pair[:, m, :], k_m, preferred_element_type=jnp....  15.6 us
    reduce_sum x2, other arithmetic, stats_of(): mass = jnp.sum(weights, axis=-1, keepdims=True)  11.4 us
    gather x1, local copies, waits for them, and re-layouts, on_device(): jnp.take(gathered.reshape(chips, span, -1), slot, axis=0, mode='clip')  10.7 us
    ppermute x2, waiting for transfers between devices, on_device(): lax.ppermute(kv_both[..., i * 2 * QK:(i + 1) * 2 * QK], 'z', [(0, 1), (1,...  10.6 us
  transfers between devices with their start and end apart: 7, of which 6 were waited for; matrix products, arithmetic and copies ran while one was open for 8% of the time, Pallas kernels for 0%

commit v1 on v0

--- a/solution.py
+++ b/solution.py
@@ -97,7 +97,8 @@
     quad = lax.dynamic_update_slice_in_dim(quad, theirs, (1 - core) * rows, axis=1)
     kv_quad = quad.reshape(2 * span, -1)
     kv_pair = lax.dynamic_index_in_dim(quad, z, axis=0, keepdims=False)
-    gathered = lax.all_gather(kv_quad, ("y", "x"), axis=0, tiled=True)
+    outgoing = jnp.stack([kv_quad] * lax.axis_size(("y", "x")))
+    gathered = jnp.concatenate(lax.all_to_all(outgoing, ("y", "x"), 0, 0), axis=0)
     query = rotate(
         jnp.dot(normed, w_query, preferred_element_type=jnp.float32).reshape(rows, heads, 2, QK),
         pos_own,

time: 297 us -> 440 us (1.48)
  waiting for transfers between devices: 173 us -> 304 us
  starting transfers between devices: 6.13 us -> 14 us
  local copies, waits for them, and re-layouts: 30.1 us -> 35.1 us
    all_to_all x0 -> x1, waiting for transfers between devices: none -> 227 us  [on_device(): lax.all_to_all(outgoing, ('y', 'x'), 0, 0)]
    all_gather x1 -> x0, waiting for transfers between devices: 94.9 us -> none  [on_device(): gathered = lax.all_gather(kv_quad, ('y', 'x'), axis=0, tiled=True)]
    all_to_all x0 -> x1, starting transfers between devices: none -> 6.79 us  [on_device(): lax.all_to_all(outgoing, ('y', 'x'), 0, 0)]
    another operation x0 -> x1, local copies, waits for them, and re-layouts: none -> 5.93 us  [on_device(): outgoing = jnp.stack([kv_quad] * lax.axis_size(('y', 'x')))]
  transfers between devices with their start and end apart: 7 -> 7, of which waited for: 6 -> 6; matrix products, arithmetic and copies ran while one was open for 8% -> 6% of each run, Pallas kernels for 0% -> 0%
where the time goes in v1:
time: 440 us; the launch traced here: 439 us
  waiting for transfers between devices  304 us (69%)
  matrix products  43.1 us (10%)
  local copies, waits for them, and re-layouts  35.1 us (8%)
  other arithmetic  28.7 us (7%)
  between operations  14.5 us (3%)
  starting transfers between devices  14 us (3%)
    all_to_all x1, waiting for transfers between devices, on_device(): lax.all_to_all(outgoing, ('y', 'x'), 0, 0)  227 us
    psum x1, waiting for transfers between devices, on_device(): lax.psum(jnp.dot(merged, w_out, preferred_element_type=jnp.float32).astyp...  64.9 us
    dot_general x6, matrix products, stats_of(): jnp.dot(weights.astype(jnp.bfloat16), v_win, preferred_element_type=jnp.f...  17 us
    dot_general x6, matrix products, stats_of(): jnp.einsum('qd,kd->qk', q_pair[:, m, :], k_m, preferred_element_type=jnp....  15.6 us
    reduce_sum x2, other arithmetic, stats_of(): mass = jnp.sum(weights, axis=-1, keepdims=True)  11.4 us
    gather x1, local copies, waits for them, and re-layouts, on_device(): jnp.take(gathered.reshape(chips, span, -1), slot, axis=0, mode='clip')  10.7 us
    ppermute x2, waiting for transfers between devices, on_device(): lax.ppermute(kv_both[..., i * 2 * QK:(i + 1) * 2 * QK], 'z', [(0, 1), (1,...  10.6 us
  transfers between devices with their start and end apart: 7, of which 6 were waited for; matrix products, arithmetic and copies ran while one was open for 6% of the time, Pallas kernels for 0%

profile of v1, /device:TPU:1, one launch (start us, length us, event | category | flops | bytes accessed | tf_op | source)
XLA Modules:
  0.0 439.3 jit_solution(17875728378917444919)
XLA Ops:
  7.2 1.0 reduce-window.8
  8.2 0.7 bitcast_subtract_fusion
  9.0 1.5 fusion.16
  10.6 2.7 fusion.131
  13.3 0.3 reshape.339
  13.6 0.5 multiply_cosine_fusion
  14.2 0.8 multiply_subtract_fusion
  15.0 0.7 maximum_convert_fusion
  15.7 0.8 fusion.136
  16.6 2.7 convolution_convert_fusion.1
  19.2 0.7 copy-done.4
  20.0 0.4 fusion.137
  20.4 0.9 copy.47
  21.4 0.8 fusion.103
  22.2 2.5 collective-permute-start.1
  24.8 5.1 %collective-permute-done.1 = bf16[256,2,256]{2,0,1:T(8,128)(2,1)S(1)} collective-permute-done((bf16[256,2,256]{2,0,1:T(8,128)(2,1)}, bf16[256,2,256]{2,0,1:T(8,128)(2,1)S(1)}, u32[]{:S(2)}, u32[]{:S(2)}) %collective-permute-start.1) | collective-permute-done | bytes 262176 | tf_op jit(solution)/shard_map/ppermute | solution.py:87
  29.9 5.5 %collective-permute-done.2 = bf16[256,2,256]{2,0,1:T(8,128)(2,1)} collective-permute-done((bf16[256,2,256]{2,0,1:T(8,128)(2,1)S(1)}, bf16[256,2,256]{2,0,1:T(8,128)(2,1)}, u32[]{:S(2)}, u32[]{:S(2)}) %collective-permute-start.2) | collective-permute-done | bytes 262176 | tf_op jit(solution)/shard_map/ppermute | solution.py:87
  35.5 1.0 maximum_dynamic-update-slice_fusion
  36.5 1.0 dynamic-slice_bitcast_fusion.1
  37.5 2.4 collective-permute-start.3
  40.0 1.1 constant_dynamic-update-slice_fusion.1
  41.1 0.7 collective-permute-done.3
  41.8 1.1 constant_dynamic-update-slice_fusion
  42.8 5.9 %stack.15 = bf16[16,1024,512]{2,1,0:T(8,128)(2,1)} broadcast(bf16[1024,512]{1,0:T(8,128)(2,1)S(1)} %bitcast.87), dimensions={1,2} | broadcast | bytes 17825792 | tf_op jit(solution)/shard_map/stack | solution.py:100
  48.8 6.8 %all-to-all-start = ((bf16[16,1024,512]{2,1,0:T(8,128)(2,1)}), bf16[16,1024,512]{2,1,0:T(8,128)(2,1)}, u32[]{:S(2)}, u32[]{:S(2)}) async-start(bf16[16,1024,512]{2,1,0:T(8,128)(2,1)} %stack.15), calls=%async_computation | async-start | bytes 33554432 | tf_op jit(solution)/shard_map/all_to_all | solution.py:101
  55.6 3.5 fusion.133
  59.1 2.2 reshape.338
  61.3 2.0 add_convert_fusion
  63.3 0.7 fusion.113
  64.1 0.7 copy.49
  64.7 0.7 collective-permute-start
  65.4 0.6 pad_clamp_fusion
  66.0 0.6 broadcast_compare_fusion
  66.8 0.6 iota_add_fusion
  67.4 1.2 convert_reduce_fusion.2
  68.6 0.5 subtract_add_fusion
  69.2 0.7 copy-done.5
  69.9 0.7 constant_dynamic-slice_fusion.2
  70.6 1.2 dynamic_slice.55
  71.8 0.9 convert_reduce_fusion.1
  72.7 1.6 constant_dynamic-update-slice_fusion.2
  74.3 1.3 fusion.139
  75.6 1.3 fusion.138
  77.0 0.4 fusion.93
  77.4 0.5 fusion.95
  78.0 1.3 fusion.97
  79.3 226.7 %all-to-all-done = bf16[16,1024,512]{2,1,0:T(8,128)(2,1)} async-done(((bf16[16,1024,512]{2,1,0:T(8,128)(2,1)}), bf16[16,1024,512]{2,1,0:T(8,128)(2,1)}, u32[]{:S(2)}, u32[]{:S(2)}) %all-to-all-start) | async-done | bytes 16777248 | tf_op jit(solution)/shard_map/all_to_all | solution.py:101
  306.0 10.7 %gather_fusion = bf16[16,512,512]{2,1,0:T(8,128)(2,1)} fusion(bf16[32,512,512]{2,1,0:T(8,128)(2,1)} %bitcast.20, s32[1024]{0:T(1024)} %pad_clamp_fusion), kind=kCustom, calls=%fused_computation | custom fusion | bytes 16777280 | tf_op jit(solution)/shard_map/jit(_take)/gather | solution.py:141
  316.6 3.9 fusion.135
  320.6 2.4 fusion.142
  322.9 2.4 fusion.141
  325.3 4.6 %fusion.143 = (f32[512]{0:T(512)S(1)}, f32[512,4096]{1,0:T(8,128)}) fusion(bf16[4096,512]{1,0:T(8,128)(2,1)S(1)} %bitcast.92, bf16[512,2,128]{2,0,1:T(8,128)(2,1)S(1)} %copy-done.6, s32[512]{0:T(512)S(1)} %copy-done.7, s32[4096]{0:T(1024)S(1)} %get-tuple-element.28, pred[4096]{0:T(1024)(128)(4,1)S(1)} %copy-done.11), kind=kOutput, calls=%fused_computation.189 | convolution fusion | flops 547356160 | bytes 9592832 | tf_op jit(solution)/shard_map/qd,kd->qk/dot_general | solution.py:125
  329.9 3.6 fusion.140
  333.5 11.0 %fusion.4 = (f32[512]{0:T(512)S(1)}, f32[512]{0:T(512)S(1)}, f32[512]{0:T(512)S(1)}, f32[512]{0:T(512)S(1)}) fusion(f32[512,4096]{1,0:T(8,128)S(1)} %get-tuple-element.64, f32[512]{0:T(512)S(1)} %get-tuple-element.63, s32[4096]{0:T(1024)S(1)} %get-tuple-element.27, s32[512]{0:T(512)S(1)} %copy-done.7, pred[4096]{0:T(1024)(128)(4,1)S(1)} %copy-done.10, ...), kind=kLoop, calls=%fused_computation.15 | loop fusion | flops 33552384 | bytes 33613824 | tf_op jit(solution)/shard_map/reduce_sum | solution.py:131
  344.5 5.6 %fusion.61 = f32[512,256]{1,0:T(8,128)S(1)} fusion(bf16[4096,512]{1,0:T(8,128)(2,1)} %bitcast.94, f32[512,4096]{1,0:T(8,128)} %get-tuple-element.68, f32[512]{0:T(512)S(1)} %get-tuple-element.67, s32[4096]{0:T(1024)S(1)} %get-tuple-element.28, s32[512]{0:T(512)S(1)} %copy-done.7, pred[4096]{0:T(1024)(128)(4,1)S(1)} %copy-done.11, f32[512]{0:T(512)S(1)} %bitcast.124), kind=kOutput, calls=%fused_computation.46 | convolution fusion | flops 1084358656 | bytes 11036672 | tf_op jit(solution)/shard_map/dot_general | solution.py:132
  350.2 3.9 fusion.41
  354.2 2.4 fusion.85
  356.6 3.1 multiply_reduce_fusion
  359.9 1.6 collective-permute-start.4
  361.5 1.0 collective-permute-done.4
  362.5 1.7 convolution_convert_fusion
  364.2 0.8 convert_element_type.86
  365.0 64.9 %all-reduce.2.cloned.1.call-done = bf16[256,2048]{1,0:T(8,128)(2,1)} async-done(((bf16[256,2048]{1,0:T(8,128)(2,1)}), bf16[256,2048]{1,0:T(8,128)(2,1)}) %all-reduce.2.cloned.1.call-update) | async-done | bytes 1048592 | tf_op jit(solution)/shard_map/psum | solution.py:184
  429.9 2.6 fusion.19
  (59 shorter events, 1.2 us)
Async XLA Ops:
  7.2 355.3 %copy-start = (bf16[512,2048]{1,0:T(8,128)(2,1)S(1)}, bf16[512,2048]{1,0:T(8,128)(2,1)}, u32[]{:S(2)}) copy-start(bf16[512,2048]{1,0:T(8,128)(2,1)} %param.14) | copy-start | bytes 6291460
  8.2 2.4 copy-start.12
  10.6 6.0 %copy-start.14 = (f32[2048]{0:T(1024)S(1)}, f32[2048]{0:T(1024)}, u32[]{:S(2)}) copy-start(f32[2048]{0:T(1024)} %param.10) | copy-start | bytes 24580
  14.2 5.9 %copy-start.3 = (f32[256,64]{1,0:T(8,128)}, f32[256,64]{1,0:T(8,128)S(1)}, u32[]{:S(2)}) copy-start(f32[256,64]{1,0:T(8,128)S(1)} %get-tuple-element.56) | copy-start | bytes 196612
  19.2 0.7 copy-start.4
  22.2 7.8 %collective-permute-start.1 = (bf16[256,2,256]{2,0,1:T(8,128)(2,1)}, bf16[256,2,256]{2,0,1:T(8,128)(2,1)S(1)}, u32[]{:S(2)}, u32[]{:S(2)}) collective-permute-start(bf16[256,2,256]{2,0,1:T(8,128)(2,1)} %get-tuple-element.47), channel_id=1, source_target_pairs={{0,32},{32,0},{1,33},{33,1},{2,34},{34,2},{3,35},{35,3},{4,36},{36... | collective-permute-start | bytes 786440 | tf_op jit(solution)/shard_map/ppermute | solution.py:87
  24.7 10.8 %collective-permute-start.2 = (bf16[256,2,256]{2,0,1:T(8,128)(2,1)S(1)}, bf16[256,2,256]{2,0,1:T(8,128)(2,1)}, u32[]{:S(2)}, u32[]{:S(2)}) collective-permute-start(bf16[256,2,256]{2,0,1:T(8,128)(2,1)S(1)} %get-tuple-element.48), channel_id=1, source_target_pairs={{0,32},{32,0},{1,33},{33,1},{2,34},{34,2},{3,35},{35,3},{4,36},{36... | collective-permute-start | bytes 786440 | tf_op jit(solution)/shard_map/ppermute | solution.py:87
  37.5 4.3 collective-permute-start.3
  48.8 257.2 %all-to-all-start = ((bf16[16,1024,512]{2,1,0:T(8,128)(2,1)}), bf16[16,1024,512]{2,1,0:T(8,128)(2,1)}, u32[]{:S(2)}, u32[]{:S(2)}) async-start(bf16[16,1024,512]{2,1,0:T(8,128)(2,1)} %stack.15), calls=%async_computation | async-start | bytes 33554432 | tf_op jit(solution)/shard_map/all_to_all | solution.py:101
  55.6 11.1 %copy-start.13 = (f32[4,2,128]{2,1,0:T(2,128)S(1)}, f32[4,2,128]{2,1,0:T(2,128)}, u32[]{:S(2)}) copy-start(f32[4,2,128]{2,1,0:T(2,128)} %param.15) | copy-start | bytes 12292
  55.6 374.3 %all-reduce.2.cloned.1.call-start = ((), (), s32[]{:S(2)}) async-start(), calls=%async_computation.1 | async-start | bytes 2097152 | tf_op jit(solution)/shard_map/psum | solution.py:184
  64.7 8.0 %collective-permute-start = (bf16[256,2,128]{2,0,1:T(8,128)(2,1)}, bf16[256,2,128]{2,0,1:T(8,128)(2,1)}, u32[]{:S(2)}, u32[]{:S(2)}) collective-permute-start(bf16[256,2,128]{2,0,1:T(8,128)(2,1)} %bitcast.86), channel_id=1, source_target_pairs={{0,4},{4,0},{1,5},{5,1},{2,6},{6,2},{3,7},{7,3},{8,12},{12,8},{9,1... | collective-permute-start | bytes 393224 | tf_op jit(solution)/shard_map/ppermute | solution.py:36
  65.4 3.7 copy-start.8
  69.2 0.7 copy-start.5
  69.9 7.0 %copy-start.7 = (s32[512]{0:T(512)S(1)}, s32[512]{0:T(512)}, u32[]{:S(2)}) copy-start(s32[512]{0:T(512)} %convert_reduce_fusion.2) | copy-start | bytes 6148
  69.9 7.0 %copy-start.9 = (s32[512]{0:T(512)S(1)}, s32[512]{0:T(512)}, u32[]{:S(2)}) copy-start(s32[512]{0:T(512)} %copy-done.8) | copy-start | bytes 6148
  316.6 3.9 copy-start.6
  316.6 3.9 copy-start.10
  320.5 4.8 %copy-start.2 = (bf16[8,512,512]{2,1,0:T(8,128)(2,1)}, bf16[8,512,512]{2,1,0:T(8,128)(2,1)S(1)}, u32[]{:S(2)}) copy-start(bf16[8,512,512]{2,1,0:T(8,128)(2,1)S(1)} %get-tuple-element.38) | copy-start | bytes 12582916
  322.9 2.4 copy-start.11
  350.2 4.0 copy-start.15
  359.7 70.2 %copy-start.1 = (bf16[256,2048]{1,0:T(8,128)(2,1)S(1)}, bf16[256,2048]{1,0:T(8,128)(2,1)}, u32[]{:S(2)}) copy-start(bf16[256,2048]{1,0:T(8,128)(2,1)} %param.9) | copy-start | bytes 3145732
  359.9 2.6 collective-permute-start.4
Sparse Core Ops, SparseCore 0:
  364.3 65.5 all-reduce.1
